TPU v7x, 128 devices: a whole 4x4x4 slice. The times are simulated.
128 devices in a mesh: dp: 16 (over y, x_lo, core), ctx: 8 (over z, x_hi).
Axes of the slice: x: 4 (x_hi: 2, x_lo: 2; x = x_hi * 2 + x_lo), y: 4, z: 4, core: 2. Of those that a mesh axis runs over, the one named last changes fastest.
Arguments:
- query_in: bfloat16 [32768, 2048], P(('dp', 'ctx')), may hold values from -16 to 16
- key_in: bfloat16 [32768, 512], P(('dp', 'ctx')), may hold values from -16 to 16
- value_in: bfloat16 [32768, 512], P(('dp', 'ctx')), may hold values from -6 to 6
- grad_out: bfloat16 [32768, 2048], P(('dp', 'ctx')), may hold values from -6 to 6
- target: int32 [32768], P(('dp', 'ctx')), may hold values from 0 to 32767, as said below
- span_order: int32 [16, 16], P('dp'), may hold values from 0 to 15, each once within a row
- doc_ids: int32 [16, 2048], P('dp', 'ctx'), may hold values from 0 to 7, never falling along the last dimension, each value on 1 to 1024 neighbouring positions
Outputs:
- grad_query: float32 [32768, 2048], P(('dp', 'ctx'))
- grad_key: float32 [32768, 512], P(('dp', 'ctx'))
- grad_value: float32 [32768, 512], P(('dp', 'ctx'))
Inputs may be any that keep to these rules, and one draw needn't show every extreme that they name: target is a permutation of the 32768 packed rows; of the 256 rows of one device at most 4 go to any one block of 256 packed rows, and exactly 4 go to some block. `span_order`: each row names every span once. `doc_ids`: each document is one run of 1 to 1024 positions; numbers never fall along a pack.
All inputs are finite; a program needn't handle non-finite values.
Results may differ from a plain program's by a relative error of at most 0.035.
Values may be sent and summed in bfloat16 or wider, within the bound.
No kernel may reach another device: no remote copies, remote signals or barrier semaphores. Data moves between devices by JAX's collectives and lax.ppermute only.
A program may use at most 128 MiB of HBM per device.

v0:
```python
import jax
import jax.numpy as jnp
from jax import lax
from jax.sharding import PartitionSpec as P

HQ = 16
HK = 4
DH = 128
block_keys = 512


def visible(query_pos, query_doc, key_pos, key_doc):
    return (key_pos[None, :] <= query_pos[:, None]) & (key_doc[None, :] == query_doc[:, None])


def masked_scores(query_blk, key_blk, allowed):
    raw_scores = jnp.einsum(
        "qhgd,khd->hgqk", query_blk, key_blk, preferred_element_type=jnp.float32
    ) * DH ** (-0.5)
    return jnp.where(allowed[None, None], raw_scores, -jnp.inf)


def grad_terms(query_blk, grad_blk, lse_blk, delta_blk, key_blk, value_blk, allowed):
    scores = masked_scores(query_blk, key_blk, allowed)
    probs = jnp.exp(scores - lse_blk[..., None])
    probs_low = probs.astype(jnp.bfloat16)
    dprobs = jnp.einsum("qhgd,khd->hgqk", grad_blk, value_blk, preferred_element_type=jnp.float32)
    dscore_low = (probs * (dprobs - delta_blk[..., None])).astype(jnp.bfloat16)
    return (probs_low, dscore_low)


def local(query_in, key_in, value_in, grad_out, target, span_order, doc_ids):
    local_rows = query_in.shape[0]
    devices = lax.axis_size(("dp", "ctx"))
    ctx_size = lax.axis_size("ctx")
    capacity = local_rows // devices + 2
    groups = HQ // HK
    score_scale = DH ** (-0.5)
    q_cols = query_in.shape[1]
    k_cols = key_in.shape[1]
    owners = target // local_rows
    onehot = (owners[:, None] == jnp.arange(devices, dtype=jnp.int32)[None, :]).astype(jnp.int32)
    earlier = jnp.cumsum(onehot, axis=0) - onehot
    slot_ids = owners * capacity + jnp.sum(earlier * onehot, axis=1)
    place_col = (
        jnp.zeros((local_rows, 128), jnp.bfloat16)
        .at[:, 0]
        .set((target % local_rows + 1).astype(jnp.bfloat16))
    )
    payload = jnp.concatenate([query_in, key_in, value_in, grad_out, place_col], axis=1)
    width = payload.shape[1]
    holder = jnp.zeros((devices * capacity, width), jnp.bfloat16).at[slot_ids].set(payload)
    got = lax.all_to_all(
        holder.reshape(devices, capacity, width),
        ("dp", "ctx"),
        split_axis=0,
        concat_axis=0,
        tiled=True,
    ).reshape(devices * capacity, width)
    arrived = got[:, 2 * q_cols + 2 * k_cols].astype(jnp.int32) - 1
    landing = jnp.where(arrived >= 0, arrived, local_rows)
    rows = jnp.zeros((local_rows, width), jnp.bfloat16).at[landing].set(got, mode="drop")
    query = rows[:, :q_cols]
    kv_rows = rows[:, q_cols : q_cols + 2 * k_cols]
    grad_rows = rows[:, q_cols + 2 * k_cols : 2 * q_cols + 2 * k_cols]
    span_rows = local_rows // 2
    span_seq = span_order[0]
    pack_len = local_rows * ctx_size
    positions = (
        span_seq[:, None] * span_rows + jnp.arange(span_rows, dtype=jnp.int32)[None, :]
    ).reshape(-1)
    ctx_index = lax.axis_index("ctx")
    own_pos = lax.dynamic_slice_in_dim(positions, ctx_index * local_rows, local_rows)
    doc_col = (
        jnp.zeros((local_rows, 128), jnp.bfloat16).at[:, 0].set(doc_ids[0].astype(jnp.bfloat16))
    )
    gathered = lax.all_gather(
        jnp.concatenate([kv_rows, doc_col], axis=1), "ctx", axis=0, tiled=True
    )
    seq_docs = gathered[:, 2 * k_cols].astype(jnp.int32)
    doc_all = seq_docs.reshape(2 * ctx_size, span_rows)[span_seq].reshape(-1)
    own_docs = lax.dynamic_slice_in_dim(doc_all, ctx_index * local_rows, local_rows)
    query_heads = query.reshape(local_rows, HK, groups, DH)
    grad_heads = grad_rows.reshape(local_rows, HK, groups, DH)
    key_heads = gathered[:, :k_cols].reshape(pack_len, HK, DH)
    value_heads = gathered[:, k_cols : 2 * k_cols].reshape(pack_len, HK, DH)
    num_blocks = pack_len // block_keys

    def key_block(block_index):
        first_key = block_index * block_keys
        return (
            lax.dynamic_slice_in_dim(key_heads, first_key, block_keys),
            lax.dynamic_slice_in_dim(value_heads, first_key, block_keys),
            lax.dynamic_slice_in_dim(positions, first_key, block_keys),
            lax.dynamic_slice_in_dim(doc_all, first_key, block_keys),
        )

    def stats_step(block_index, carry):
        key_blk, value_blk, key_pos, key_doc = key_block(block_index)
        allowed = visible(own_pos, own_docs, key_pos, key_doc)
        running_max, running_sum = carry
        scores = masked_scores(query_heads, key_blk, allowed)
        new_max = jnp.maximum(running_max, jnp.max(scores, axis=-1))
        rescale = jnp.exp(running_max - new_max)
        running_sum = running_sum * rescale + jnp.sum(jnp.exp(scores - new_max[..., None]), axis=-1)
        return (new_max, running_sum)

    start_stats = (
        jnp.full((HK, groups, local_rows), -1e30, jnp.float32),
        jnp.zeros((HK, groups, local_rows), jnp.float32),
    )
    running_max, running_sum = lax.fori_loop(0, num_blocks, stats_step, start_stats)
    log_norm = running_max + jnp.log(running_sum)

    def output_step(block_index, carry):
        key_blk, value_blk, key_pos, key_doc = key_block(block_index)
        allowed = visible(own_pos, own_docs, key_pos, key_doc)
        scores = masked_scores(query_heads, key_blk, allowed)
        probs_low = jnp.exp(scores - log_norm[..., None]).astype(jnp.bfloat16)
        return carry + jnp.einsum(
            "hgqk,khd->qhgd", probs_low, value_blk, preferred_element_type=jnp.float32
        )

    summed = lax.fori_loop(
        0, num_blocks, output_step, jnp.zeros((local_rows, HK, groups, DH), jnp.float32)
    )
    attended_low = summed.astype(jnp.bfloat16)
    delta = jnp.sum(
        grad_heads.astype(jnp.float32) * attended_low.astype(jnp.float32), axis=-1
    ).transpose(1, 2, 0)

    def back_step(block_index, carry):
        key_blk, value_blk, key_pos, key_doc = key_block(block_index)
        allowed = visible(own_pos, own_docs, key_pos, key_doc)
        dquery, dkey_all, dvalue_all = carry
        probs_low, dscore_low = grad_terms(
            query_heads, grad_heads, log_norm, delta, key_blk, value_blk, allowed
        )
        dquery = dquery + jnp.einsum(
            "hgqk,khd->qhgd", dscore_low, key_blk, preferred_element_type=jnp.float32
        )
        dkey = (
            jnp.einsum(
                "hgqk,qhgd->khd", dscore_low, query_heads, preferred_element_type=jnp.float32
            )
            * score_scale
        )
        dvalue = jnp.einsum(
            "hgqk,qhgd->khd", probs_low, grad_heads, preferred_element_type=jnp.float32
        )
        first_key = block_index * block_keys
        dkey_all = lax.dynamic_update_slice_in_dim(
            dkey_all, dkey.reshape(block_keys, HK * DH), first_key, 0
        )
        dvalue_all = lax.dynamic_update_slice_in_dim(
            dvalue_all, dvalue.reshape(block_keys, HK * DH), first_key, 0
        )
        return (dquery, dkey_all, dvalue_all)

    start_back = (
        jnp.zeros((local_rows, HK, groups, DH), jnp.float32),
        jnp.zeros((pack_len, HK * DH), jnp.float32),
        jnp.zeros((pack_len, HK * DH), jnp.float32),
    )
    dquery, dkey_all, dvalue_all = lax.fori_loop(0, num_blocks, back_step, start_back)
    partial = jnp.concatenate([dkey_all, dvalue_all], axis=1).astype(jnp.bfloat16)
    summed_kv = jnp.sum(
        lax.all_to_all(
            partial.reshape(ctx_size, local_rows, 2 * k_cols),
            "ctx",
            split_axis=0,
            concat_axis=0,
            tiled=True,
        ).astype(jnp.float32),
        axis=0,
    )
    dquery_full = (dquery * score_scale).reshape(local_rows, HQ * DH)
    source_rows = jnp.where(arrived >= 0, arrived, 0)
    result = jnp.concatenate(
        [dquery_full.astype(jnp.bfloat16), summed_kv.astype(jnp.bfloat16)], axis=1
    )
    back = (
        lax.all_to_all(
            result[source_rows].reshape(devices, capacity, q_cols + 2 * k_cols),
            ("dp", "ctx"),
            split_axis=0,
            concat_axis=0,
            tiled=True,
        )
        .reshape(devices * capacity, q_cols + 2 * k_cols)[slot_ids]
        .astype(jnp.float32)
    )
    return (back[:, :q_cols], back[:, q_cols : q_cols + k_cols], back[:, q_cols + k_cols :])


def solution(mesh):
    placed = (
        P(("dp", "ctx"), None),
        P(("dp", "ctx"), None),
        P(("dp", "ctx"), None),
        P(("dp", "ctx"), None),
        P(("dp", "ctx")),
        P("dp", None),
        P("dp", "ctx"),
    )
    return jax.shard_map(
        local,
        mesh=mesh,
        in_specs=placed,
        out_specs=(P(("dp", "ctx"), None), P(("dp", "ctx"), None), P(("dp", "ctx"), None)),
        check_vma=False,
    )
```

profile of v0, /device:TPU:1, one launch (start us, length us, event | category | flops | bytes accessed | tf_op | source)
XLA Modules:
  0.0 499.3 jit_solution(9435614256057329827)
XLA Ops:
  11.9 2.4 constant_dynamic-update-slice_fusion.5
  17.6 8.6 %scatter_custom_fusion = bf16[512,5248]{1,0:T(8,128)(2,1)} fusion(s32[256]{0:T(256)S(1)} %compare_select_fusion.4, bf16[256,5248]{1,0:T(8,128)(2,1)} %pad_dynamic-update-slice_fusion, bf16[]{:T(256)} %constant.226.clone.1), kind=kCustom, calls=%fused_computation.63 | custom fusion | bytes 5374464 | tf_op jit(solution)/shard_map/scatter | solution.py:52
  26.2 9.4 %reshape.352 = bf16[128,4,5248]{2,1,0:T(4,128)(2,1)} reshape(bf16[512,5248]{1,0:T(8,128)(2,1)} %scatter_custom_fusion) | data formatting | bytes 10747904 | tf_op jit(solution)/shard_map/reshape | solution.py:54
  35.6 11.9 %all-to-all-start = ((bf16[128,4,5248]{2,1,0:T(4,128)(2,1)}), bf16[128,4,5248]{2,1,0:T(4,128)(2,1)}, u32[]{:S(2)}, u32[]{:S(2)}) async-start(bf16[128,4,5248]{2,1,0:T(4,128)(2,1)} %reshape.352), calls=%async_computation | async-start | bytes 10747904 | tf_op jit(solution)/shard_map/all_to_all | solution.py:53
  48.9 64.2 %all-to-all-done = bf16[128,4,5248]{2,1,0:T(4,128)(2,1)} async-done(((bf16[128,4,5248]{2,1,0:T(4,128)(2,1)}), bf16[128,4,5248]{2,1,0:T(4,128)(2,1)}, u32[]{:S(2)}, u32[]{:S(2)}) %all-to-all-start) | async-done | bytes 5373984 | tf_op jit(solution)/shard_map/all_to_all | solution.py:53
  113.1 9.0 %reshape.399 = bf16[512,5248]{1,0:T(8,128)(2,1)} reshape(bf16[128,4,5248]{2,1,0:T(4,128)(2,1)} %all-to-all-done) | data formatting | bytes 10747904 | tf_op jit(solution)/shard_map/reshape | solution.py:59
  123.9 10.3 %scatter_custom_fusion.1 = bf16[256,5248]{1,0:T(8,128)(2,1)S(1)} fusion(s32[512]{0:T(512)S(1)} %get-tuple-element.848, bf16[512,5248]{1,0:T(8,128)(2,1)} %reshape.399, bf16[]{:T(256)} %constant.226.clone.1), kind=kCustom, calls=%fused_computation.68 | custom fusion | bytes 2687488 | tf_op jit(solution)/shard_map/scatter | solution.py:62
  136.1 2.7 fusion.68
  142.0 2.4 copy.108
  146.7 59.6 %all-gather.2.cloned.1.call-done = bf16[2048,1152]{1,0:T(8,128)(2,1)} async-done(((bf16[256,1152]{1,0:T(8,128)(2,1)}), bf16[2048,1152]{1,0:T(8,128)(2,1)}) %all-gather.2.cloned.1.call-update) | async-done | bytes 4718608 | tf_op jit(solution)/shard_map/all_gather | solution.py:77
  206.3 4.5 fusion.67
  210.9 4.0 copy.103
  216.9 4.0 copy.100
  220.8 3.9 copy.107
  224.8 18.0 %while.50 = (s32[]{:T(128)}, f32[4,4,256]{2,1,0:T(4,128)S(1)}, f32[4,4,256]{2,1,0:T(4,128)S(1)}, s32[2048]{0:T(1024)S(1)}, s32[256]{0:T(256)S(1)}, /*index=5*/s3...) while((s32[]{:T(128)}, f32[4,4,256]{2,1,0:T(4,128)S(1)}, ...), condition=%wide.region_9.10_spmd.clone, body=%wide.region_6.9_spmd.clone.sunk | while | flops 551964672 | bytes 18970824 | solution.py:112
  242.8 23.8 %while.51 = (s32[]{:T(128)}, f32[256,4,4,128]{0,3,2,1:T(8,128)}, bf16[2048,4,128]{0,2,1:T(8,128)(2,1)}, s32[2048]{0:T(1024)S(1)}, s32[256]{0:T(256)S(1)}, /*inde...) while((s32[]{:T(128)}, f32[256,4,4,128]{0,3,2,1:T(8,128)}, ...), condition=%wide.region_11.12_spmd.clone, body=%wide.region_10.11_spmd.clone.sunk | while | flops 1083572224 | bytes 6586060 | solution.py:124
  243.2 5.0 %bitcast_add_fusion.4 = f32[256,4,4,128]{0,3,2,1:T(8,128)} fusion(f32[256,4,4,128]{0,3,2,1:T(8,128)} %get-tuple-element.1188, f32[4,4,256]{2,1,0:T(4,128)S(1)} %get-tuple-element.1210, pred[256,512]{0,1:T(8,128)(4,1)S(1)} %compare_and_fusion.7, bf16[256,4,4,128]{3,0,2,1:T(8,128)(2,1)S(1)} %get-tuple-element.1209, pred[]{:T(512)S(6)} %compare.35, ...), kind=kOutput, calls=%fused_computation.26.clone.1 | convolution fusion | flops 1083179008 | bytes 6440448 | tf_op jit(solution)/shard_map/while/body/eval_jaxpr/hgqk,khd->qhgd/dot_general | solution.py:120
  248.6 5.8 %bitcast_add_fusion.4 = f32[256,4,4,128]{0,3,2,1:T(8,128)} fusion(f32[256,4,4,128]{0,3,2,1:T(8,128)} %get-tuple-element.1188, f32[4,4,256]{2,1,0:T(4,128)S(1)} %get-tuple-element.1210, pred[256,512]{0,1:T(8,128)(4,1)S(1)} %compare_and_fusion.7, bf16[256,4,4,128]{3,0,2,1:T(8,128)(2,1)S(1)} %get-tuple-element.1209, pred[]{:T(512)S(6)} %compare.35, ...), kind=kOutput, calls=%fused_computation.26.clone.1 | convolution fusion | flops 1083179008 | bytes 6440448 | tf_op jit(solution)/shard_map/while/body/eval_jaxpr/hgqk,khd->qhgd/dot_general | solution.py:120
  254.8 5.8 %bitcast_add_fusion.4 = f32[256,4,4,128]{0,3,2,1:T(8,128)} fusion(f32[256,4,4,128]{0,3,2,1:T(8,128)} %get-tuple-element.1188, f32[4,4,256]{2,1,0:T(4,128)S(1)} %get-tuple-element.1210, pred[256,512]{0,1:T(8,128)(4,1)S(1)} %compare_and_fusion.7, bf16[256,4,4,128]{3,0,2,1:T(8,128)(2,1)S(1)} %get-tuple-element.1209, pred[]{:T(512)S(6)} %compare.35, ...), kind=kOutput, calls=%fused_computation.26.clone.1 | convolution fusion | flops 1083179008 | bytes 6440448 | tf_op jit(solution)/shard_map/while/body/eval_jaxpr/hgqk,khd->qhgd/dot_general | solution.py:120
  260.9 5.8 %bitcast_add_fusion.4 = f32[256,4,4,128]{0,3,2,1:T(8,128)} fusion(f32[256,4,4,128]{0,3,2,1:T(8,128)} %get-tuple-element.1188, f32[4,4,256]{2,1,0:T(4,128)S(1)} %get-tuple-element.1210, pred[256,512]{0,1:T(8,128)(4,1)S(1)} %compare_and_fusion.7, bf16[256,4,4,128]{3,0,2,1:T(8,128)(2,1)S(1)} %get-tuple-element.1209, pred[]{:T(512)S(6)} %compare.35, ...), kind=kOutput, calls=%fused_computation.26.clone.1 | convolution fusion | flops 1083179008 | bytes 6440448 | tf_op jit(solution)/shard_map/while/body/eval_jaxpr/hgqk,khd->qhgd/dot_general | solution.py:120
  271.7 82.2 %while.52 = (s32[]{:T(128)}, f32[256,4,4,128]{0,3,2,1:T(8,128)S(1)}, bf16[2048,512]{1,0:T(8,128)(2,1)}, bf16[2048,512]{1,0:T(8,128)(2,1)}, bf16[2048,4,128]{2,0,...) while((s32[]{:T(128)}, ...), condition=%wide.region_14.15_spmd.clone, body=%wide.region_13.14_spmd.clone.sunk | while | flops 2707292160 | bytes 74381608 | solution.py:165
  272.3 2.7 fusion.117
  277.3 5.3 %fusion.118 = bf16[4,4,256,512]{2,3,1,0:T(8,128)(2,1)} fusion(f32[4,512,256,4]{2,1,3,0:T(8,128)S(1)} %fusion.117, f32[4,4,256]{2,1,0:T(4,128)S(1)} %get-tuple-element.1264, f32[4,4,256]{2,1,0:T(4,128)S(1)} %get-tuple-element.1261, pred[256,512]{0,1:T(8,128)(4,1)S(1)} %compare_and_fusion.8, bf16[256,4,4,128]{0,3,2,1:T(8,128)(2,1)S(1)} %copy-done.3, ...), kind=kOutput, calls=%fused_computation.37.clone.1 | convolution fusion | flops 549453824 | bytes 14319620 | tf_op jit(solution)/shard_map/while/body/eval_jaxpr/qhgd,khd->hgqk/dot_general | solution.py:27
  282.9 4.9 fusion.120
  287.8 2.4 bitcast_add_fusion.5
  292.8 2.7 fusion.117
  297.8 5.3 %fusion.118 = bf16[4,4,256,512]{2,3,1,0:T(8,128)(2,1)} fusion(f32[4,512,256,4]{2,1,3,0:T(8,128)S(1)} %fusion.117, f32[4,4,256]{2,1,0:T(4,128)S(1)} %get-tuple-element.1264, f32[4,4,256]{2,1,0:T(4,128)S(1)} %get-tuple-element.1261, pred[256,512]{0,1:T(8,128)(4,1)S(1)} %compare_and_fusion.8, bf16[256,4,4,128]{0,3,2,1:T(8,128)(2,1)S(1)} %copy-done.3, ...), kind=kOutput, calls=%fused_computation.37.clone.1 | convolution fusion | flops 549453824 | bytes 14319620 | tf_op jit(solution)/shard_map/while/body/eval_jaxpr/qhgd,khd->hgqk/dot_general | solution.py:27
  303.4 4.9 fusion.120
  308.3 2.4 bitcast_add_fusion.5
  313.3 2.7 fusion.117
  318.3 5.3 %fusion.118 = bf16[4,4,256,512]{2,3,1,0:T(8,128)(2,1)} fusion(f32[4,512,256,4]{2,1,3,0:T(8,128)S(1)} %fusion.117, f32[4,4,256]{2,1,0:T(4,128)S(1)} %get-tuple-element.1264, f32[4,4,256]{2,1,0:T(4,128)S(1)} %get-tuple-element.1261, pred[256,512]{0,1:T(8,128)(4,1)S(1)} %compare_and_fusion.8, bf16[256,4,4,128]{0,3,2,1:T(8,128)(2,1)S(1)} %copy-done.3, ...), kind=kOutput, calls=%fused_computation.37.clone.1 | convolution fusion | flops 549453824 | bytes 14319620 | tf_op jit(solution)/shard_map/while/body/eval_jaxpr/qhgd,khd->hgqk/dot_general | solution.py:27
  323.9 4.9 fusion.120
  328.8 2.4 bitcast_add_fusion.5
  333.8 2.7 fusion.117
  338.8 5.3 %fusion.118 = bf16[4,4,256,512]{2,3,1,0:T(8,128)(2,1)} fusion(f32[4,512,256,4]{2,1,3,0:T(8,128)S(1)} %fusion.117, f32[4,4,256]{2,1,0:T(4,128)S(1)} %get-tuple-element.1264, f32[4,4,256]{2,1,0:T(4,128)S(1)} %get-tuple-element.1261, pred[256,512]{0,1:T(8,128)(4,1)S(1)} %compare_and_fusion.8, bf16[256,4,4,128]{0,3,2,1:T(8,128)(2,1)S(1)} %copy-done.3, ...), kind=kOutput, calls=%fused_computation.37.clone.1 | convolution fusion | flops 549453824 | bytes 14319620 | tf_op jit(solution)/shard_map/while/body/eval_jaxpr/qhgd,khd->hgqk/dot_general | solution.py:27
  344.4 4.9 fusion.120
  349.3 2.4 bitcast_add_fusion.5
  354.0 4.7 pad_maximum_fusion
  358.6 6.4 %copy.114 = bf16[8,256,1024]{1,2,0:T(8,128)(2,1)} copy(bf16[8,256,1024]{2,1,0:T(8,128)(2,1)} %pad_maximum_fusion) | data formatting | bytes 8388608 | tf_op jit(solution)/shard_map/concatenate | solution.py:166
  365.1 4.7 all-to-all-start.1
  370.7 48.7 %all-to-all-done.1 = bf16[8,256,1024]{1,2,0:T(8,128)(2,1)} async-done(((bf16[8,256,1024]{1,2,0:T(8,128)(2,1)}), bf16[8,256,1024]{1,2,0:T(8,128)(2,1)}, u32[]{:S(2)}, u32[]{:S(2)}) %all-to-all-start.1) | async-done | bytes 4194336 | tf_op jit(solution)/shard_map/all_to_all | solution.py:168
  419.4 3.0 reduce_sum.45
  422.8 3.9 gather_fusion.1
  426.6 6.1 %reshape.360 = bf16[128,4,3072]{2,1,0:T(4,128)(2,1)} reshape(bf16[512,3072]{1,0:T(8,128)(2,1)} %gather_fusion.1) | data formatting | bytes 6291456 | tf_op jit(solution)/shard_map/reshape | solution.py:184
  432.8 7.5 %all-to-all-start.2 = ((bf16[128,4,3072]{2,1,0:T(4,128)(2,1)}), bf16[128,4,3072]{2,1,0:T(4,128)(2,1)}, u32[]{:S(2)}, u32[]{:S(2)}) async-start(bf16[128,4,3072]{2,1,0:T(4,128)(2,1)} %reshape.360), calls=%async_computation.2 | async-start | bytes 6291456 | tf_op jit(solution)/shard_map/all_to_all | solution.py:183
  440.3 40.9 %all-to-all-done.2 = bf16[128,4,3072]{2,1,0:T(4,128)(2,1)} async-done(((bf16[128,4,3072]{2,1,0:T(4,128)(2,1)}), bf16[128,4,3072]{2,1,0:T(4,128)(2,1)}, u32[]{:S(2)}, u32[]{:S(2)}) %all-to-all-start.2) | async-done | bytes 3145760 | tf_op jit(solution)/shard_map/all_to_all | solution.py:183
  481.2 4.5 reshape.361
  485.7 2.7 gather_fusion.2
  (161 shorter events, 70.3 us)
Async XLA Ops:
  7.2 7.2 %copy-start.5 = (bf16[256,512]{1,0:T(8,128)(2,1)S(1)}, bf16[256,512]{1,0:T(8,128)(2,1)}, u32[]{:S(2)}) copy-start(bf16[256,512]{1,0:T(8,128)(2,1)} %param.18) | copy-start | bytes 786436
  7.2 7.9 %copy-start.6 = (bf16[256,512]{1,0:T(8,128)(2,1)S(1)}, bf16[256,512]{1,0:T(8,128)(2,1)}, u32[]{:S(2)}) copy-start(bf16[256,512]{1,0:T(8,128)(2,1)} %param.19) | copy-start | bytes 786436
  7.2 8.7 %copy-start.4 = (bf16[256,2048]{1,0:T(8,128)(2,1)S(1)}, bf16[256,2048]{1,0:T(8,128)(2,1)}, u32[]{:S(2)}) copy-start(bf16[256,2048]{1,0:T(8,128)(2,1)} %param.20) | copy-start | bytes 3145732
  11.9 5.6 %copy-start.8 = (s32[256]{0:T(256)}, s32[256]{0:T(256)S(1)}, u32[]{:S(2)}) copy-start(s32[256]{0:T(256)S(1)} %compare_select_fusion.4) | copy-start | bytes 3076
  35.6 12.5 %copy-start.10 = (s32[1,256]{1,0:T(1,128)S(1)}, s32[1,256]{1,0:T(1,128)}, u32[]{:S(2)}) copy-start(s32[1,256]{1,0:T(1,128)} %param.23) | copy-start | bytes 3076
  35.6 77.5 %all-to-all-start = ((bf16[128,4,5248]{2,1,0:T(4,128)(2,1)}), bf16[128,4,5248]{2,1,0:T(4,128)(2,1)}, u32[]{:S(2)}, u32[]{:S(2)}) async-start(bf16[128,4,5248]{2,1,0:T(4,128)(2,1)} %reshape.352), calls=%async_computation | async-start | bytes 10747904 | tf_op jit(solution)/shard_map/all_to_all | solution.py:53
  47.5 158.8 %all-gather.2.cloned.1.call-start = ((), (), s32[]{:S(2)}) async-start(), calls=%async_computation.3 | async-start | bytes 5308416 | tf_op jit(solution)/shard_map/all_gather | solution.py:77
  123.9 12.1 %copy-start.11 = (s32[1,16]{1,0:T(1,128)S(1)}, s32[1,16]{1,0:T(1,128)}, u32[]{:S(2)}) copy-start(s32[1,16]{1,0:T(1,128)} %param.22) | copy-start | bytes 196
  134.2 1.7 copy-start.2
  272.3 2.7 copy-start.3
  282.8 4.9 copy-start
  292.8 2.7 copy-start.3
  303.3 4.9 copy-start
  313.3 2.7 copy-start.3
  323.9 4.9 copy-start
  333.8 2.7 copy-start.3
  344.4 4.9 copy-start
  365.1 4.7 copy-start.7
  365.1 54.3 %all-to-all-start.1 = ((bf16[8,256,1024]{1,2,0:T(8,128)(2,1)}), bf16[8,256,1024]{1,2,0:T(8,128)(2,1)}, u32[]{:S(2)}, u32[]{:S(2)}) async-start(bf16[8,256,1024]{1,2,0:T(8,128)(2,1)} %copy.114), calls=%async_computation.1 | async-start | bytes 8388608 | tf_op jit(solution)/shard_map/all_to_all | solution.py:168
  432.8 7.5 %copy-start.9 = (s32[256]{0:T(256)S(1)}, s32[256]{0:T(256)}, u32[]{:S(2)}) copy-start(s32[256]{0:T(256)} %copy-done.8) | copy-start | bytes 3076
  432.8 48.4 %all-to-all-start.2 = ((bf16[128,4,3072]{2,1,0:T(4,128)(2,1)}), bf16[128,4,3072]{2,1,0:T(4,128)(2,1)}, u32[]{:S(2)}, u32[]{:S(2)}) async-start(bf16[128,4,3072]{2,1,0:T(4,128)(2,1)} %reshape.360), calls=%async_computation.2 | async-start | bytes 6291456 | tf_op jit(solution)/shard_map/all_to_all | solution.py:183
  488.4 2.3 copy-start.1
Sparse Core Ops, SparseCore 0:
  135.4 70.8 all-gather.1
where the time goes:
time: 508 us; the launch traced here: 499 us
  waiting for transfers between devices  213 us (42%)
  local copies, waits for them, and re-layouts  115 us (23%)
  matrix products  102 us (20%)
  other arithmetic  29 us (6%)
  starting transfers between devices  24.6 us (5%)
  between operations  14.6 us (3%)
    all_to_all x1, waiting for transfers between devices, local(): lax.all_to_all(holder.reshape(devices, capacity, width), ('dp', 'ctx'), s...  64.2 us
    all_gather x1, waiting for transfers between devices, local(): lax.all_gather(jnp.concatenate([kv_rows, doc_col], axis=1), 'ctx', axis=0...  59.6 us
    all_to_all x1, waiting for transfers between devices, local(): lax.all_to_all(partial.reshape(ctx_size, local_rows, 2 * k_cols), 'ctx',...  48.7 us
    all_to_all x1, waiting for transfers between devices, local(): lax.all_to_all(result[source_rows].reshape(devices, capacity, q_cols + 2...  40.9 us
    dot_general x4, matrix products, output_step(): jnp.einsum('hgqk,khd->qhgd', probs_low, value_blk, preferred_element_type...  22.3 us
    dot_general x4, matrix products, grad_terms(): jnp.einsum('qhgd,khd->hgqk', grad_blk, value_blk, preferred_element_type=...  21.3 us
    dot_general x8, matrix products, masked_scores(): jnp.einsum('qhgd,khd->hgqk', query_blk, key_blk, preferred_element_type=j...  20.3 us
    dot_general x4, matrix products, back_step(): jnp.einsum('hgqk,qhgd->khd', dscore_low, query_heads, preferred_element_t...  19.7 us
  transfers between devices with their start and end apart: 4, of which 4 were waited for; matrix products, arithmetic and copies ran while one was open for 2% of the time, Pallas kernels for 0%

commit v1 on v0

--- a/solution.py
+++ b/solution.py
@@ -74,8 +74,14 @@
     doc_col = (
         jnp.zeros((local_rows, 128), jnp.bfloat16).at[:, 0].set(doc_ids[0].astype(jnp.bfloat16))
     )
-    gathered = lax.all_gather(
-        jnp.concatenate([kv_rows, doc_col], axis=1), "ctx", axis=0, tiled=True
+    gathered = jnp.concatenate(
+        lax.all_to_all(
+            jnp.stack([jnp.concatenate([kv_rows, doc_col], axis=1)] * lax.axis_size("ctx")),
+            "ctx",
+            0,
+            0,
+        ),
+        axis=0,
     )
     seq_docs = gathered[:, 2 * k_cols].astype(jnp.int32)
     doc_all = seq_docs.reshape(2 * ctx_size, span_rows)[span_seq].reshape(-1)

time: 508 us -> 479 us (0.943)
  waiting for transfers between devices: 213 us -> 196 us
  between operations: 14.6 us -> 1.21 us
    all_gather x1 -> x0, waiting for transfers between devices: 59.6 us -> none  [local(): lax.all_gather(jnp.concatenate([kv_rows, doc_col], axis=1), 'ctx', axis=0...]
    all_to_all x0 -> x1, waiting for transfers between devices: none -> 44.3 us  [local(): lax.all_to_all(jnp.stack([jnp.concatenate([kv_rows, doc_col], axis=1)] *...]
    slice x2 -> x1, local copies, waits for them, and re-layouts: 8.49 us -> 2.29 us  [local(): value_heads = gathered[:, k_cols:2 * k_cols].reshape(pack_len, HK, DH)]
  transfers between devices with their start and end apart: 4 -> 4, of which waited for: 4 -> 4; matrix products, arithmetic and copies ran while one was open for 2% -> 3% of each run, Pallas kernels for 0% -> 0%
where the time goes in v1:
time: 479 us; the launch traced here: 470 us
  waiting for transfers between devices  196 us (41%)
  local copies, waits for them, and re-layouts  113 us (24%)
  matrix products  102 us (21%)
  starting transfers between devices  29.6 us (6%)
  other arithmetic  27.7 us (6%)
    all_to_all x1, waiting for transfers between devices, local(): lax.all_to_all(holder.reshape(devices, capacity, width), ('dp', 'ctx'), s...  64.5 us
    all_to_all x1, waiting for transfers between devices, local(): lax.all_to_all(partial.reshape(ctx_size, local_rows, 2 * k_cols), 'ctx',...  46.4 us
    all_to_all x1, waiting for transfers between devices, local(): lax.all_to_all(jnp.stack([jnp.concatenate([kv_rows, doc_col], axis=1)] *...  44.3 us
    all_to_all x1, waiting for transfers between devices, local(): lax.all_to_all(result[source_rows].reshape(devices, capacity, q_cols + 2...  41 us
    dot_general x4, matrix products, output_step(): jnp.einsum('hgqk,khd->qhgd', probs_low, value_blk, preferred_element_type...  22.3 us
    dot_general x4, matrix products, grad_terms(): jnp.einsum('qhgd,khd->hgqk', grad_blk, value_blk, preferred_element_type=...  21.2 us
    dot_general x8, matrix products, masked_scores(): jnp.einsum('qhgd,khd->hgqk', query_blk, key_blk, preferred_element_type=j...  20.3 us
    dot_general x4, matrix products, back_step(): jnp.einsum('hgqk,qhgd->khd', dscore_low, query_heads, preferred_element_t...  19.7 us
  transfers between devices with their start and end apart: 4, of which 4 were waited for; matrix products, arithmetic and copies ran while one was open for 3% of the time, Pallas kernels for 0%

profile of v1, /device:TPU:1, one launch (start us, length us, event | category | flops | bytes accessed | tf_op | source)
XLA Modules:
  0.0 470.4 jit_solution(13478414303771620035)
XLA Ops:
  5.4 2.4 constant_dynamic-update-slice_fusion.5
  11.1 8.6 %scatter_custom_fusion = bf16[512,5248]{1,0:T(8,128)(2,1)} fusion(s32[256]{0:T(256)S(1)} %compare_select_fusion.4, bf16[256,5248]{1,0:T(8,128)(2,1)} %pad_dynamic-update-slice_fusion, bf16[]{:T(256)} %constant.226.clone.1), kind=kCustom, calls=%fused_computation.63 | custom fusion | bytes 5374464 | tf_op jit(solution)/shard_map/scatter | solution.py:52
  19.6 9.4 %reshape.357 = bf16[128,4,5248]{2,1,0:T(4,128)(2,1)} reshape(bf16[512,5248]{1,0:T(8,128)(2,1)} %scatter_custom_fusion) | data formatting | bytes 10747904 | tf_op jit(solution)/shard_map/reshape | solution.py:54
  29.1 12.6 %all-to-all-start = ((bf16[128,4,5248]{2,1,0:T(4,128)(2,1)}), bf16[128,4,5248]{2,1,0:T(4,128)(2,1)}, u32[]{:S(2)}, u32[]{:S(2)}) async-start(bf16[128,4,5248]{2,1,0:T(4,128)(2,1)} %reshape.357), calls=%async_computation | async-start | bytes 10747904 | tf_op jit(solution)/shard_map/all_to_all | solution.py:53
  42.5 64.5 %all-to-all-done = bf16[128,4,5248]{2,1,0:T(4,128)(2,1)} async-done(((bf16[128,4,5248]{2,1,0:T(4,128)(2,1)}), bf16[128,4,5248]{2,1,0:T(4,128)(2,1)}, u32[]{:S(2)}, u32[]{:S(2)}) %all-to-all-start) | async-done | bytes 5373984 | tf_op jit(solution)/shard_map/all_to_all | solution.py:53
  107.0 9.0 %reshape.405 = bf16[512,5248]{1,0:T(8,128)(2,1)} reshape(bf16[128,4,5248]{2,1,0:T(4,128)(2,1)} %all-to-all-done) | data formatting | bytes 10747904 | tf_op jit(solution)/shard_map/reshape | solution.py:59
  117.2 10.2 %scatter_custom_fusion.1 = bf16[256,5248]{1,0:T(8,128)(2,1)S(1)} fusion(s32[512]{0:T(512)S(1)} %get-tuple-element.848, bf16[512,5248]{1,0:T(8,128)(2,1)} %reshape.405, bf16[]{:T(256)} %constant.226.clone.1), kind=kCustom, calls=%fused_computation.68 | custom fusion | bytes 2687488 | tf_op jit(solution)/shard_map/scatter | solution.py:62
  128.8 3.5 stack.2
  132.4 4.9 %all-to-all-start.1 = ((bf16[8,256,1152]{1,2,0:T(8,128)(2,1)}), bf16[8,256,1152]{1,2,0:T(8,128)(2,1)}, u32[]{:S(2)}, u32[]{:S(2)}) async-start(bf16[8,256,1152]{1,2,0:T(8,128)(2,1)} %stack.2), calls=%async_computation.1 | async-start | bytes 9437184 | tf_op jit(solution)/shard_map/all_to_all | solution.py:78
  137.5 2.8 fusion.68
  143.3 2.4 copy.106
  148.6 44.3 %all-to-all-done.1 = bf16[8,256,1152]{1,2,0:T(8,128)(2,1)} async-done(((bf16[8,256,1152]{1,2,0:T(8,128)(2,1)}), bf16[8,256,1152]{1,2,0:T(8,128)(2,1)}, u32[]{:S(2)}, u32[]{:S(2)}) %all-to-all-start.1) | async-done | bytes 4718624 | tf_op jit(solution)/shard_map/all_to_all | solution.py:78
  192.9 3.0 copy.141
  198.2 4.0 copy.105
  202.8 18.0 %while.50 = (s32[]{:T(128)}, f32[4,4,256]{2,1,0:T(4,128)S(1)}, f32[4,4,256]{2,1,0:T(4,128)S(1)}, s32[2048]{0:T(1024)S(1)}, s32[256]{0:T(256)S(1)}, /*index=5*/s3...) while((s32[]{:T(128)}, f32[4,4,256]{2,1,0:T(4,128)S(1)}, ...), condition=%wide.region_9.10_spmd.clone, body=%wide.region_6.9_spmd.clone.sunk | while | flops 551964672 | bytes 18970824 | solution.py:118
  220.9 23.8 %while.51 = (s32[]{:T(128)}, f32[256,4,4,128]{0,3,2,1:T(8,128)}, bf16[2048,4,128]{0,2,1:T(8,128)(2,1)}, s32[2048]{0:T(1024)S(1)}, s32[256]{0:T(256)S(1)}, /*inde...) while((s32[]{:T(128)}, f32[256,4,4,128]{0,3,2,1:T(8,128)}, ...), condition=%wide.region_11.12_spmd.clone, body=%wide.region_10.11_spmd.clone.sunk | while | flops 1083572224 | bytes 6586060 | solution.py:130
  221.3 5.0 %bitcast_add_fusion.4 = f32[256,4,4,128]{0,3,2,1:T(8,128)} fusion(f32[256,4,4,128]{0,3,2,1:T(8,128)} %get-tuple-element.1190, f32[4,4,256]{2,1,0:T(4,128)S(1)} %get-tuple-element.1212, pred[256,512]{0,1:T(8,128)(4,1)S(1)} %compare_and_fusion.7, bf16[256,4,4,128]{3,0,2,1:T(8,128)(2,1)S(1)} %get-tuple-element.1211, pred[]{:T(512)S(6)} %compare.35, ...), kind=kOutput, calls=%fused_computation.26.clone.1 | convolution fusion | flops 1083179008 | bytes 6440448 | tf_op jit(solution)/shard_map/while/body/eval_jaxpr/hgqk,khd->qhgd/dot_general | solution.py:126
  226.7 5.8 %bitcast_add_fusion.4 = f32[256,4,4,128]{0,3,2,1:T(8,128)} fusion(f32[256,4,4,128]{0,3,2,1:T(8,128)} %get-tuple-element.1190, f32[4,4,256]{2,1,0:T(4,128)S(1)} %get-tuple-element.1212, pred[256,512]{0,1:T(8,128)(4,1)S(1)} %compare_and_fusion.7, bf16[256,4,4,128]{3,0,2,1:T(8,128)(2,1)S(1)} %get-tuple-element.1211, pred[]{:T(512)S(6)} %compare.35, ...), kind=kOutput, calls=%fused_computation.26.clone.1 | convolution fusion | flops 1083179008 | bytes 6440448 | tf_op jit(solution)/shard_map/while/body/eval_jaxpr/hgqk,khd->qhgd/dot_general | solution.py:126
  232.8 5.8 %bitcast_add_fusion.4 = f32[256,4,4,128]{0,3,2,1:T(8,128)} fusion(f32[256,4,4,128]{0,3,2,1:T(8,128)} %get-tuple-element.1190, f32[4,4,256]{2,1,0:T(4,128)S(1)} %get-tuple-element.1212, pred[256,512]{0,1:T(8,128)(4,1)S(1)} %compare_and_fusion.7, bf16[256,4,4,128]{3,0,2,1:T(8,128)(2,1)S(1)} %get-tuple-element.1211, pred[]{:T(512)S(6)} %compare.35, ...), kind=kOutput, calls=%fused_computation.26.clone.1 | convolution fusion | flops 1083179008 | bytes 6440448 | tf_op jit(solution)/shard_map/while/body/eval_jaxpr/hgqk,khd->qhgd/dot_general | solution.py:126
  238.9 5.8 %bitcast_add_fusion.4 = f32[256,4,4,128]{0,3,2,1:T(8,128)} fusion(f32[256,4,4,128]{0,3,2,1:T(8,128)} %get-tuple-element.1190, f32[4,4,256]{2,1,0:T(4,128)S(1)} %get-tuple-element.1212, pred[256,512]{0,1:T(8,128)(4,1)S(1)} %compare_and_fusion.7, bf16[256,4,4,128]{3,0,2,1:T(8,128)(2,1)S(1)} %get-tuple-element.1211, pred[]{:T(512)S(6)} %compare.35, ...), kind=kOutput, calls=%fused_computation.26.clone.1 | convolution fusion | flops 1083179008 | bytes 6440448 | tf_op jit(solution)/shard_map/while/body/eval_jaxpr/hgqk,khd->qhgd/dot_general | solution.py:126
  249.8 82.1 %while.52 = (s32[]{:T(128)}, f32[256,4,4,128]{0,3,2,1:T(8,128)S(1)}, bf16[2048,512]{1,0:T(8,128)(2,1)}, bf16[2048,512]{1,0:T(8,128)(2,1)}, bf16[2048,4,128]{2,0,...) while((s32[]{:T(128)}, ...), condition=%wide.region_14.15_spmd.clone, body=%wide.region_13.14_spmd.clone.sunk | while | flops 2707292160 | bytes 74381608 | solution.py:171
  250.4 2.7 fusion.117
  255.4 5.3 %fusion.118 = bf16[4,4,256,512]{2,3,1,0:T(8,128)(2,1)} fusion(f32[4,512,256,4]{2,1,3,0:T(8,128)S(1)} %fusion.117, f32[4,4,256]{2,1,0:T(4,128)S(1)} %get-tuple-element.1266, f32[4,4,256]{2,1,0:T(4,128)S(1)} %get-tuple-element.1263, pred[256,512]{0,1:T(8,128)(4,1)S(1)} %compare_and_fusion.8, bf16[256,4,4,128]{0,3,2,1:T(8,128)(2,1)S(1)} %copy-done.3, ...), kind=kOutput, calls=%fused_computation.37.clone.1 | convolution fusion | flops 549453824 | bytes 14319620 | tf_op jit(solution)/shard_map/while/body/eval_jaxpr/qhgd,khd->hgqk/dot_general | solution.py:27
  260.9 4.9 %fusion.120 = bf16[4,512,128]{1,2,0:T(8,128)(2,1)} fusion(bf16[4,4,256,512]{2,3,1,0:T(8,128)(2,1)} %fusion.118, bf16[256,4,4,128]{0,3,2,1:T(8,128)(2,1)} %get-tuple-element.1262), kind=kOutput, calls=%fused_computation.46.clone.1 | convolution fusion | flops 537395200 | bytes 5767168 | tf_op jit(solution)/shard_map/while/body/eval_jaxpr/hgqk,qhgd->khd/dot_general | solution.py:149
  265.8 2.4 bitcast_add_fusion.5
  270.9 2.7 fusion.117
  275.9 5.3 %fusion.118 = bf16[4,4,256,512]{2,3,1,0:T(8,128)(2,1)} fusion(f32[4,512,256,4]{2,1,3,0:T(8,128)S(1)} %fusion.117, f32[4,4,256]{2,1,0:T(4,128)S(1)} %get-tuple-element.1266, f32[4,4,256]{2,1,0:T(4,128)S(1)} %get-tuple-element.1263, pred[256,512]{0,1:T(8,128)(4,1)S(1)} %compare_and_fusion.8, bf16[256,4,4,128]{0,3,2,1:T(8,128)(2,1)S(1)} %copy-done.3, ...), kind=kOutput, calls=%fused_computation.37.clone.1 | convolution fusion | flops 549453824 | bytes 14319620 | tf_op jit(solution)/shard_map/while/body/eval_jaxpr/qhgd,khd->hgqk/dot_general | solution.py:27
  281.4 4.9 %fusion.120 = bf16[4,512,128]{1,2,0:T(8,128)(2,1)} fusion(bf16[4,4,256,512]{2,3,1,0:T(8,128)(2,1)} %fusion.118, bf16[256,4,4,128]{0,3,2,1:T(8,128)(2,1)} %get-tuple-element.1262), kind=kOutput, calls=%fused_computation.46.clone.1 | convolution fusion | flops 537395200 | bytes 5767168 | tf_op jit(solution)/shard_map/while/body/eval_jaxpr/hgqk,qhgd->khd/dot_general | solution.py:149
  286.3 2.4 bitcast_add_fusion.5
  291.3 2.7 fusion.117
  296.3 5.3 %fusion.118 = bf16[4,4,256,512]{2,3,1,0:T(8,128)(2,1)} fusion(f32[4,512,256,4]{2,1,3,0:T(8,128)S(1)} %fusion.117, f32[4,4,256]{2,1,0:T(4,128)S(1)} %get-tuple-element.1266, f32[4,4,256]{2,1,0:T(4,128)S(1)} %get-tuple-element.1263, pred[256,512]{0,1:T(8,128)(4,1)S(1)} %compare_and_fusion.8, bf16[256,4,4,128]{0,3,2,1:T(8,128)(2,1)S(1)} %copy-done.3, ...), kind=kOutput, calls=%fused_computation.37.clone.1 | convolution fusion | flops 549453824 | bytes 14319620 | tf_op jit(solution)/shard_map/while/body/eval_jaxpr/qhgd,khd->hgqk/dot_general | solution.py:27
  301.8 4.9 %fusion.120 = bf16[4,512,128]{1,2,0:T(8,128)(2,1)} fusion(bf16[4,4,256,512]{2,3,1,0:T(8,128)(2,1)} %fusion.118, bf16[256,4,4,128]{0,3,2,1:T(8,128)(2,1)} %get-tuple-element.1262), kind=kOutput, calls=%fused_computation.46.clone.1 | convolution fusion | flops 537395200 | bytes 5767168 | tf_op jit(solution)/shard_map/while/body/eval_jaxpr/hgqk,qhgd->khd/dot_general | solution.py:149
  306.8 2.4 bitcast_add_fusion.5
  311.8 2.7 fusion.117
  316.8 5.3 %fusion.118 = bf16[4,4,256,512]{2,3,1,0:T(8,128)(2,1)} fusion(f32[4,512,256,4]{2,1,3,0:T(8,128)S(1)} %fusion.117, f32[4,4,256]{2,1,0:T(4,128)S(1)} %get-tuple-element.1266, f32[4,4,256]{2,1,0:T(4,128)S(1)} %get-tuple-element.1263, pred[256,512]{0,1:T(8,128)(4,1)S(1)} %compare_and_fusion.8, bf16[256,4,4,128]{0,3,2,1:T(8,128)(2,1)S(1)} %copy-done.3, ...), kind=kOutput, calls=%fused_computation.37.clone.1 | convolution fusion | flops 549453824 | bytes 14319620 | tf_op jit(solution)/shard_map/while/body/eval_jaxpr/qhgd,khd->hgqk/dot_general | solution.py:27
  322.3 4.9 %fusion.120 = bf16[4,512,128]{1,2,0:T(8,128)(2,1)} fusion(bf16[4,4,256,512]{2,3,1,0:T(8,128)(2,1)} %fusion.118, bf16[256,4,4,128]{0,3,2,1:T(8,128)(2,1)} %get-tuple-element.1262), kind=kOutput, calls=%fused_computation.46.clone.1 | convolution fusion | flops 537395200 | bytes 5767168 | tf_op jit(solution)/shard_map/while/body/eval_jaxpr/hgqk,qhgd->khd/dot_general | solution.py:149
  327.2 2.4 bitcast_add_fusion.5
  331.9 4.7 pad_maximum_fusion
  336.6 6.4 %copy.112 = bf16[8,256,1024]{1,2,0:T(8,128)(2,1)} copy(bf16[8,256,1024]{2,1,0:T(8,128)(2,1)} %pad_maximum_fusion) | data formatting | bytes 8388608 | tf_op jit(solution)/shard_map/concatenate | solution.py:172
  343.1 4.5 all-to-all-start.2
  350.3 46.4 %all-to-all-done.2 = bf16[8,256,1024]{1,2,0:T(8,128)(2,1)} async-done(((bf16[8,256,1024]{1,2,0:T(8,128)(2,1)}), bf16[8,256,1024]{1,2,0:T(8,128)(2,1)}, u32[]{:S(2)}, u32[]{:S(2)}) %all-to-all-start.2) | async-done | bytes 4194336 | tf_op jit(solution)/shard_map/all_to_all | solution.py:174
  396.8 3.0 reduce_sum.45
  400.5 3.8 gather_fusion.1
  404.4 6.1 %reshape.366 = bf16[128,4,3072]{2,1,0:T(4,128)(2,1)} reshape(bf16[512,3072]{1,0:T(8,128)(2,1)} %gather_fusion.1) | data formatting | bytes 6291456 | tf_op jit(solution)/shard_map/reshape | solution.py:190
  410.5 7.6 %all-to-all-start.3 = ((bf16[128,4,3072]{2,1,0:T(4,128)(2,1)}), bf16[128,4,3072]{2,1,0:T(4,128)(2,1)}, u32[]{:S(2)}, u32[]{:S(2)}) async-start(bf16[128,4,3072]{2,1,0:T(4,128)(2,1)} %reshape.366), calls=%async_computation.3 | async-start | bytes 6291456 | tf_op jit(solution)/shard_map/all_to_all | solution.py:189
  418.1 41.0 %all-to-all-done.3 = bf16[128,4,3072]{2,1,0:T(4,128)(2,1)} async-done(((bf16[128,4,3072]{2,1,0:T(4,128)(2,1)}), bf16[128,4,3072]{2,1,0:T(4,128)(2,1)}, u32[]{:S(2)}, u32[]{:S(2)}) %all-to-all-start.3) | async-done | bytes 3145760 | tf_op jit(solution)/shard_map/all_to_all | solution.py:189
  459.1 4.5 reshape.367
  463.6 2.7 gather_fusion.2
  (160 shorter events, 72.4 us)
Async XLA Ops:
  0.6 7.2 %copy-start.5 = (bf16[256,512]{1,0:T(8,128)(2,1)S(1)}, bf16[256,512]{1,0:T(8,128)(2,1)}, u32[]{:S(2)}) copy-start(bf16[256,512]{1,0:T(8,128)(2,1)} %param.18) | copy-start | bytes 786436
  0.6 7.9 %copy-start.6 = (bf16[256,512]{1,0:T(8,128)(2,1)S(1)}, bf16[256,512]{1,0:T(8,128)(2,1)}, u32[]{:S(2)}) copy-start(bf16[256,512]{1,0:T(8,128)(2,1)} %param.19) | copy-start | bytes 786436
  0.7 8.7 %copy-start.4 = (bf16[256,2048]{1,0:T(8,128)(2,1)S(1)}, bf16[256,2048]{1,0:T(8,128)(2,1)}, u32[]{:S(2)}) copy-start(bf16[256,2048]{1,0:T(8,128)(2,1)} %param.20) | copy-start | bytes 3145732
  5.4 5.6 %copy-start.8 = (s32[256]{0:T(256)}, s32[256]{0:T(256)S(1)}, u32[]{:S(2)}) copy-start(s32[256]{0:T(256)S(1)} %compare_select_fusion.4) | copy-start | bytes 3076
  29.1 12.6 %copy-start.10 = (s32[1,256]{1,0:T(1,128)S(1)}, s32[1,256]{1,0:T(1,128)}, u32[]{:S(2)}) copy-start(s32[1,256]{1,0:T(1,128)} %param.23) | copy-start | bytes 3076
  29.1 77.9 %all-to-all-start = ((bf16[128,4,5248]{2,1,0:T(4,128)(2,1)}), bf16[128,4,5248]{2,1,0:T(4,128)(2,1)}, u32[]{:S(2)}, u32[]{:S(2)}) async-start(bf16[128,4,5248]{2,1,0:T(4,128)(2,1)} %reshape.357), calls=%async_computation | async-start | bytes 10747904 | tf_op jit(solution)/shard_map/all_to_all | solution.py:53
  127.3 5.0 %copy-start.2 = (bf16[256,5248]{1,0:T(8,128)(2,1)}, bf16[256,5248]{1,0:T(8,128)(2,1)S(1)}, u32[]{:S(2)}) copy-start(bf16[256,5248]{1,0:T(8,128)(2,1)S(1)} %scatter_custom_fusion.1) | copy-start | bytes 8060932
  132.4 4.9 %copy-start.11 = (s32[1,16]{1,0:T(1,128)S(1)}, s32[1,16]{1,0:T(1,128)}, u32[]{:S(2)}) copy-start(s32[1,16]{1,0:T(1,128)} %param.22) | copy-start | bytes 196
  132.4 60.6 %all-to-all-start.1 = ((bf16[8,256,1152]{1,2,0:T(8,128)(2,1)}), bf16[8,256,1152]{1,2,0:T(8,128)(2,1)}, u32[]{:S(2)}, u32[]{:S(2)}) async-start(bf16[8,256,1152]{1,2,0:T(8,128)(2,1)} %stack.2), calls=%async_computation.1 | async-start | bytes 9437184 | tf_op jit(solution)/shard_map/all_to_all | solution.py:78
  250.4 2.7 copy-start.3
  260.9 4.9 %copy-start = (bf16[4,4,256,512]{2,3,1,0:T(8,128)(2,1)S(1)}, bf16[4,4,256,512]{2,3,1,0:T(8,128)(2,1)}, u32[]{:S(2)}) copy-start(bf16[4,4,256,512]{2,3,1,0:T(8,128)(2,1)} %fusion.118) | copy-start | bytes 12582916 | tf_op jit(solution)/shard_map/while
  270.9 2.7 copy-start.3
  281.4 4.9 %copy-start = (bf16[4,4,256,512]{2,3,1,0:T(8,128)(2,1)S(1)}, bf16[4,4,256,512]{2,3,1,0:T(8,128)(2,1)}, u32[]{:S(2)}) copy-start(bf16[4,4,256,512]{2,3,1,0:T(8,128)(2,1)} %fusion.118) | copy-start | bytes 12582916 | tf_op jit(solution)/shard_map/while
  291.3 2.7 copy-start.3
  301.8 4.9 %copy-start = (bf16[4,4,256,512]{2,3,1,0:T(8,128)(2,1)S(1)}, bf16[4,4,256,512]{2,3,1,0:T(8,128)(2,1)}, u32[]{:S(2)}) copy-start(bf16[4,4,256,512]{2,3,1,0:T(8,128)(2,1)} %fusion.118) | copy-start | bytes 12582916 | tf_op jit(solution)/shard_map/while
  311.8 2.7 copy-start.3
  322.3 4.9 %copy-start = (bf16[4,4,256,512]{2,3,1,0:T(8,128)(2,1)S(1)}, bf16[4,4,256,512]{2,3,1,0:T(8,128)(2,1)}, u32[]{:S(2)}) copy-start(bf16[4,4,256,512]{2,3,1,0:T(8,128)(2,1)} %fusion.118) | copy-start | bytes 12582916 | tf_op jit(solution)/shard_map/while
  343.1 53.7 %all-to-all-start.2 = ((bf16[8,256,1024]{1,2,0:T(8,128)(2,1)}), bf16[8,256,1024]{1,2,0:T(8,128)(2,1)}, u32[]{:S(2)}, u32[]{:S(2)}) async-start(bf16[8,256,1024]{1,2,0:T(8,128)(2,1)} %copy.112), calls=%async_computation.2 | async-start | bytes 8388608 | tf_op jit(solution)/shard_map/all_to_all | solution.py:174
  399.8 0.7 copy-start.7
  410.5 7.6 %copy-start.9 = (s32[256]{0:T(256)S(1)}, s32[256]{0:T(256)}, u32[]{:S(2)}) copy-start(s32[256]{0:T(256)} %copy-done.8) | copy-start | bytes 3076
  410.5 48.7 %all-to-all-start.3 = ((bf16[128,4,3072]{2,1,0:T(4,128)(2,1)}), bf16[128,4,3072]{2,1,0:T(4,128)(2,1)}, u32[]{:S(2)}, u32[]{:S(2)}) async-start(bf16[128,4,3072]{2,1,0:T(4,128)(2,1)} %reshape.366), calls=%async_computation.3 | async-start | bytes 6291456 | tf_op jit(solution)/shard_map/all_to_all | solution.py:189
  466.3 2.3 copy-start.1
